TPU v7x, 256 devices: a whole 4x4x8 slice. The times are simulated.
256 devices in a mesh: group: 16 (over y_hi, x, core), leaf: 16 (over y_lo, z).
Axes of the slice: x: 4, y: 4 (y_hi: 2, y_lo: 2; y = y_hi * 2 + y_lo), z: 8, core: 2. Of those that a mesh axis runs over, the one named last changes fastest.
Arguments:
- leaf_mass: bfloat16 [256, 512, 512], P(('group', 'leaf')), may hold values from -23 to 23, as said below
- leaf_damp: bfloat16 [256, 512, 512], P(('group', 'leaf')), may hold values from -12 to 12, as said below
- mass_coupling: bfloat16 [256, 512, 1536], P(('group', 'leaf')), may hold values from -6 to 6
- damp_coupling: bfloat16 [256, 512, 1536], P(('group', 'leaf')), may hold values from -6 to 6
- leaf_modes: bfloat16 [256, 512, 1536], P(('group', 'leaf')), may hold values from -0.15625 to 0.15625
- interface_blocks: int32 [256, 12], P(('group', 'leaf')), may hold values from 0 to 11, each once within a row
- mid_modes: bfloat16 [16, 1536, 256], P('group', 'leaf'), may hold values from -0.15625 to 0.15625
- mid_constraint: bfloat16 [16, 1536, 1024], P('group', 'leaf'), may hold values from -0.109375 to 0.109375
Outputs:
- coupling_mass: float32 [256, 512, 256], P(('group', 'leaf'))
- coupling_damp: float32 [256, 512, 256], P(('group', 'leaf'))
- modal_mass: float32 [16, 256, 1280], P('group', 'leaf')
- modal_damp: float32 [16, 256, 1280], P('group', 'leaf')
- root_mass: float32 [1024, 1024], P(('group', 'leaf'))
- root_damp: float32 [1024, 1024], P(('group', 'leaf'))
Inputs may be any that keep to these rules, and one draw needn't show every extreme that they name: `interface_blocks`: each row is a permutation of 0 to 11. `leaf_mass`: each leaf's block is symmetric. `leaf_damp`: each leaf's block is symmetric.
All inputs are finite; a program needn't handle non-finite values.
Results may differ from a plain program's by a relative error of at most 0.0049.
Values may be sent and summed in bfloat16 or wider, within the bound.
No kernel may reach another device: no remote copies, remote signals or barrier semaphores. Data moves between devices by JAX's collectives and lax.ppermute only.
A program may use at most 128 MiB of HBM per device.

v0:
```python
import jax
import jax.numpy as jnp
from jax import lax
from jax.sharding import PartitionSpec as P


def to_middle(stacked, onehot, block_count, block_size):
    rows_total, width_total = stacked.shape
    moved = jnp.einsum(
        "lbk,bj->ljk",
        stacked.reshape(rows_total, block_count, block_size),
        onehot,
        preferred_element_type=jnp.float32,
    )
    return moved.astype(jnp.bfloat16).reshape(rows_total, width_total)


def left_product(first_operand, second_operand):
    return lax.dot_general(
        first_operand, second_operand, (((0,), (0,)), ((), ())), preferred_element_type=jnp.float32
    )


def body(
    leaf_mass,
    leaf_damp,
    mass_coupling,
    damp_coupling,
    leaf_modes,
    interface_blocks,
    mid_modes,
    mid_constraint,
):
    leaf_order = leaf_mass.shape[1]
    block_count = interface_blocks.shape[1]
    sep_width = leaf_modes.shape[2]
    block_size = sep_width // block_count
    mode_count = mid_modes.shape[2]
    root_width = mid_constraint.shape[2]
    basis_width = mode_count + root_width
    leaf_count = lax.axis_size("leaf")
    group_count = lax.axis_size("group")
    onehot = (
        interface_blocks[0][:, None] == jnp.arange(block_count, dtype=jnp.int32)[None, :]
    ).astype(jnp.bfloat16)
    placed = to_middle(
        jnp.concatenate([leaf_modes[0], mass_coupling[0], damp_coupling[0]], axis=0),
        onehot,
        block_count,
        block_size,
    )
    constraint = placed[:leaf_order]
    sides = placed[leaf_order:].astype(jnp.float32)
    product = jnp.dot(
        jnp.concatenate([leaf_mass[0], leaf_damp[0]], axis=0),
        constraint,
        preferred_element_type=jnp.float32,
    )
    half_work = (0.5 * product + sides).astype(jnp.bfloat16)
    full_work = (product + sides).astype(jnp.bfloat16)
    basis_rows = jnp.concatenate([mid_modes[0], mid_constraint[0]], axis=1)
    mode_basis = lax.all_gather(basis_rows, "leaf", axis=0, tiled=True)
    left_sum = jnp.dot(constraint, mode_basis, preferred_element_type=jnp.float32)
    right_sum = jnp.dot(half_work, mode_basis, preferred_element_type=jnp.float32)
    coupling = jnp.dot(full_work, mode_basis[:, :mode_count], preferred_element_type=jnp.float32)
    left_part = left_sum.astype(jnp.bfloat16)
    right_part = right_sum.astype(jnp.bfloat16)
    right_mass = right_part[:leaf_order]
    right_damp = right_part[leaf_order:]

    def projected_rows(first_row, amount, first_col):
        left_rows = lax.dynamic_slice_in_dim(left_part, first_row, amount, 1)
        right_rows = lax.dynamic_slice_in_dim(right_part, first_row, amount, 1)
        left_cols = left_part[:, first_col:]
        mass_term = left_product(left_rows, right_mass[:, first_col:]) + left_product(
            right_rows[:leaf_order], left_cols
        )
        damp_term = left_product(left_rows, right_damp[:, first_col:]) + left_product(
            right_rows[leaf_order:], left_cols
        )
        return jnp.concatenate([mass_term, damp_term], axis=1)

    modal_part = lax.psum_scatter(
        projected_rows(jnp.int32(0), mode_count // leaf_count * lax.axis_size("leaf"), 0),
        "leaf",
        scatter_dimension=0,
        tiled=True,
    )
    root_part = lax.psum_scatter(
        projected_rows(
            jnp.int32(0) + mode_count,
            root_width // (group_count * leaf_count) * lax.axis_size(("group", "leaf")),
            mode_count,
        ),
        ("group", "leaf"),
        scatter_dimension=0,
        tiled=True,
    )
    return (
        coupling[:leaf_order][None],
        coupling[leaf_order:][None],
        modal_part[:, :basis_width][None],
        modal_part[:, basis_width:][None],
        root_part[:, :root_width],
        root_part[:, root_width:],
    )


def solution(mesh):
    return jax.shard_map(
        body,
        mesh=mesh,
        in_specs=(
            P(("group", "leaf"), None, None),
            P(("group", "leaf"), None, None),
            P(("group", "leaf"), None, None),
            P(("group", "leaf"), None, None),
            P(("group", "leaf"), None, None),
            P(("group", "leaf"), None),
            P("group", "leaf", None),
            P("group", "leaf", None),
        ),
        out_specs=(
            P(("group", "leaf"), None, None),
            P(("group", "leaf"), None, None),
            P("group", "leaf", None),
            P("group", "leaf", None),
            P(("group", "leaf"), None),
            P(("group", "leaf"), None),
        ),
        check_vma=False,
    )
```

profile of v0, /device:TPU:2, one launch (start us, length us, event | category | flops | bytes accessed | tf_op | source)
XLA Modules:
  0.0 474.5 jit_solution(488696714255146082)
XLA Ops:
  7.2 1.6 pad_maximum_fusion.2
  8.9 1.7 copy.41
  10.7 3.0 copy.44
  14.4 3.0 copy.45
  18.2 3.0 copy.43
  21.2 4.6 fusion
  25.8 1.2 copy.58
  27.1 2.2 copy-done.3
  29.4 0.7 copy.47
  30.1 5.2 %slice_convert_fusion = f32[1024,12,128]{2,0,1:T(8,128)} fusion(bf16[1536,12,128]{2,0,1:T(8,128)(2,1)} %bitcast.34), kind=kLoop, calls=%fused_computation.13 | loop fusion | flops 1572864 | bytes 9437184 | tf_op jit(solution)/shard_map/convert_element_type | solution.py:53
  35.3 6.6 %copy.48 = f32[1024,12,128]{0,2,1:T(8,128)} copy(f32[1024,12,128]{2,0,1:T(8,128)} %slice_convert_fusion) | data formatting | bytes 12582912 | tf_op jit(solution)/shard_map/convert_element_type | solution.py:53
  41.9 6.7 %copy.49 = f32[1024,1536]{1,0:T(8,128)} copy(f32[1024,1536]{0,1:T(8,128)} %bitcast.32) | data formatting | bytes 12582912 | tf_op jit(solution)/shard_map/convert_element_type | solution.py:53
  48.6 4.5 fusion.13
  53.0 35.5 %all-gather.2.cloned.1.call-done = bf16[1536,1280]{1,0:T(8,128)(2,1)} async-done(((bf16[96,1280]{1,0:T(8,128)(2,1)}), bf16[1536,1280]{1,0:T(8,128)(2,1)}) %all-gather.2.cloned.1.call-update) | async-done | bytes 3932176 | tf_op jit(solution)/shard_map/all_gather | solution.py:62
  88.6 4.5 convolution_convert_fusion.1
  93.1 1.3 copy-done.4
  94.4 6.6 %convolution_convert_fusion = bf16[1024,1280]{1,0:T(8,128)(2,1)S(1)} fusion(bf16[1536,1280]{1,0:T(8,128)(2,1)} %all-gather.2.cloned.1.call-done, f32[1024,1536]{1,0:T(8,128)S(1)} %copy-done.2, f32[1024,1536]{1,0:T(8,128)S(1)} %copy-done.4), kind=kOutput, calls=%fused_computation.11 | convolution fusion | flops 4032561152 | bytes 19136512 | tf_op jit(solution)/shard_map/dot_general | solution.py:64
  101.0 1.3 fusion.18
  102.3 1.3 fusion.21
  103.7 1.4 convolution_add_fusion.2
  105.1 1.4 convolution_add_fusion.3
  106.5 4.1 pad_maximum_fusion
  110.7 2.0 fusion.9
  114.4 1.8 pad_maximum_fusion.1
  116.2 6.3 %fusion.7 = f32[1024,256]{1,0:T(8,128)S(1)} fusion(f32[1024,1536]{1,0:T(8,128)} %fusion.13, f32[1024,1536]{1,0:T(8,128)} %copy.49, bf16[1536,1280]{1,0:T(8,128)(2,1)} %all-gather.2.cloned.1.call-done), kind=kOutput, calls=%fused_computation.12 | convolution fusion | flops 808452096 | bytes 14417920 | tf_op jit(solution)/shard_map/dot_general | solution.py:65
  122.5 1.0 slice_bitcast_fusion
  123.5 265.2 %all-reduce.3.cloned.1.call-done = f32[1024,2048]{0,1:T(8,128)} async-done(((f32[1024,2048]{0,1:T(8,128)}), f32[1024,2048]{0,1:T(8,128)}) %all-reduce.3.cloned.1.call-update) | async-done | bytes 8388624
  388.7 1.5 fusion.38
  390.2 0.8 copy.52
  391.0 0.8 copy.51
  391.8 74.5 %reduce-scatter.3.cloned.1.call-done = f32[16,2560]{1,0:T(8,128)} async-done(((f32[256,2560]{1,0:T(8,128)}), f32[16,2560]{1,0:T(8,128)}) %reduce-scatter.3.cloned.1.call-update) | async-done | bytes 163856 | tf_op jit(solution)/shard_map/reduce_scatter | solution.py:83
  466.3 1.6 slice_bitcast_fusion.2
  (30 shorter events, 3.4 us)
Async XLA Ops:
  7.2 81.4 %all-gather.2.cloned.1.call-start = ((), (), s32[]{:S(2)}) async-start(), calls=%async_computation.1 | async-start | bytes 4177920 | tf_op jit(solution)/shard_map/all_gather | solution.py:62
  8.9 379.8 %all-reduce.3.cloned.1.call-start = ((), (), s32[]{:S(2)}) async-start(), calls=%async_computation.3 | async-start | bytes 16777216
  10.7 3.0 copy-start.5
  14.4 3.0 copy-start.6
  18.2 3.0 copy-start.9
  27.1 2.2 copy-start.3
  41.9 6.7 %copy-start.7 = (bf16[1,512,512]{2,1,0:T(8,128)(2,1)S(1)}, bf16[1,512,512]{2,1,0:T(8,128)(2,1)}, u32[]{:S(2)}) copy-start(bf16[1,512,512]{2,1,0:T(8,128)(2,1)} %param.9) | copy-start | bytes 1572868
  41.9 6.7 %copy-start.8 = (bf16[1,512,512]{2,1,0:T(8,128)(2,1)S(1)}, bf16[1,512,512]{2,1,0:T(8,128)(2,1)}, u32[]{:S(2)}) copy-start(bf16[1,512,512]{2,1,0:T(8,128)(2,1)} %param.8) | copy-start | bytes 1572868
  88.6 4.5 copy-start.2
  88.6 5.8 %copy-start.4 = (f32[1024,1536]{1,0:T(8,128)S(1)}, f32[1024,1536]{1,0:T(8,128)}, u32[]{:S(2)}) copy-start(f32[1024,1536]{1,0:T(8,128)} %fusion.13) | copy-start | bytes 18874372
  101.0 4.1 copy-start
  110.6 355.8 %reduce-scatter.3.cloned.1.call-start = ((), (), s32[]{:S(2)}) async-start(), calls=%async_computation.2 | async-start | bytes 2785280 | tf_op jit(solution)/shard_map/reduce_scatter | solution.py:83
  110.6 2.1 copy-start.1
Sparse Core Ops, SparseCore 0:
  10.3 78.1 all-gather.1
  110.7 277.9 all-reduce.2
  391.3 75.0 reduce-scatter.2
where the time goes:
time: 475 us; the launch traced here: 474 us
  waiting for transfers between devices  375 us (79%)
  local copies, waits for them, and re-layouts  36.9 us (8%)
  matrix products  35.6 us (7%)
  between operations  13.9 us (3%)
  other arithmetic  12.6 us (3%)
    unnamed x4, waiting for transfers between devices  265 us
    reduce_scatter x1, waiting for transfers between devices, body(): lax.psum_scatter(projected_rows(jnp.int32(0), mode_count // leaf_count *...  74.5 us
    all_gather x1, waiting for transfers between devices, body(): mode_basis = lax.all_gather(basis_rows, 'leaf', axis=0, tiled=True)  35.5 us
    convert_element_type x2, local copies, waits for them, and re-layouts, body(): sides = placed[leaf_order:].astype(jnp.float32)  13.3 us
  transfers between devices with their start and end apart: 3, of which 3 were waited for; matrix products, arithmetic and copies ran while one was open for 12% of the time, Pallas kernels for 0%

commit v1 on v0

--- a/solution.py
+++ b/solution.py
@@ -59,7 +59,16 @@
     half_work = (0.5 * product + sides).astype(jnp.bfloat16)
     full_work = (product + sides).astype(jnp.bfloat16)
     basis_rows = jnp.concatenate([mid_modes[0], mid_constraint[0]], axis=1)
-    mode_basis = lax.all_gather(basis_rows, "leaf", axis=0, tiled=True)
+    block_group = lambda my_data: jnp.concatenate(
+        lax.all_to_all(
+            jnp.stack([my_data] * lax.axis_size("leaf"), 0),
+            axis_name="leaf",
+            split_axis=0,
+            concat_axis=0,
+        ),
+        0,
+    )
+    mode_basis = block_group(basis_rows)
     left_sum = jnp.dot(constraint, mode_basis, preferred_element_type=jnp.float32)
     right_sum = jnp.dot(half_work, mode_basis, preferred_element_type=jnp.float32)
     coupling = jnp.dot(full_work, mode_basis[:, :mode_count], preferred_element_type=jnp.float32)

time: 475 us -> 431 us (0.907)
  waiting for transfers between devices: 375 us -> 320 us
  starting transfers between devices: 0.12 us -> 9.84 us
    reduce_scatter x1, waiting for transfers between devices: 74.5 us -> 0.01 us  [body(): lax.psum_scatter(projected_rows(jnp.int32(0), mode_count // leaf_count *...]
    all_to_all x0 -> x1, waiting for transfers between devices: none -> 46.5 us  [body(): lax.all_to_all(jnp.stack([my_data] * lax.axis_size('leaf'), 0), axis_name...]
    all_gather x1 -> x0, waiting for transfers between devices: 35.5 us -> none  [body(): mode_basis = lax.all_gather(basis_rows, 'leaf', axis=0, tiled=True)]
    all_to_all x0 -> x1, starting transfers between devices: none -> 9.76 us  [body(): lax.all_to_all(jnp.stack([my_data] * lax.axis_size('leaf'), 0), axis_name...]
    unnamed x4 -> x3, waiting for transfers between devices: 265 us -> 273 us
  transfers between devices with their start and end apart: 3 -> 3, of which waited for: 3 -> 2; matrix products, arithmetic and copies ran while one was open for 12% -> 13% of each run, Pallas kernels for 0% -> 0%
where the time goes in v1:
time: 431 us; the launch traced here: 430 us
  waiting for transfers between devices  320 us (74%)
  local copies, waits for them, and re-layouts  38.1 us (9%)
  matrix products  35 us (8%)
  between operations  15.7 us (4%)
  other arithmetic  11.9 us (3%)
  starting transfers between devices  9.84 us (2%)
    unnamed x3, waiting for transfers between devices  273 us
    all_to_all x1, waiting for transfers between devices, body(): lax.all_to_all(jnp.stack([my_data] * lax.axis_size('leaf'), 0), axis_name...  46.5 us
    convert_element_type x2, local copies, waits for them, and re-layouts, body(): sides = placed[leaf_order:].astype(jnp.float32)  13.2 us
    all_to_all x1, starting transfers between devices, body(): lax.all_to_all(jnp.stack([my_data] * lax.axis_size('leaf'), 0), axis_name...  9.76 us
    concatenate x3, local copies, waits for them, and re-layouts, body(): jnp.concatenate([leaf_modes[0], mass_coupling[0], damp_coupling[0]], axis=0)  9.09 us
    dot_general x8, matrix products, left_product(): lax.dot_general(first_operand, second_operand, (((0,), (0,)), ((), ())),...  9.03 us
  transfers between devices with their start and end apart: 3, of which 2 were waited for; matrix products, arithmetic and copies ran while one was open for 13% of the time, Pallas kernels for 0%

profile of v1, /device:TPU:2, one launch (start us, length us, event | category | flops | bytes accessed | tf_op | source)
XLA Modules:
  0.0 430.3 jit_solution(2127604607598748169)
XLA Ops:
  8.0 0.9 pad_maximum_fusion.2
  8.9 2.3 stack.2
  11.2 9.8 %all-to-all-start = ((bf16[16,96,1280]{2,1,0:T(8,128)(2,1)}), bf16[16,96,1280]{2,1,0:T(8,128)(2,1)}, u32[]{:S(2)}, u32[]{:S(2)}) async-start(bf16[16,96,1280]{2,1,0:T(8,128)(2,1)} %stack.2), calls=%async_computation | async-start | bytes 7864320 | tf_op jit(solution)/shard_map/all_to_all | solution.py:63
  21.0 0.7 copy.41
  21.8 3.0 copy.44
  25.5 3.0 copy.45
  29.3 3.0 copy.43
  32.3 4.6 %fusion = bf16[12,1536,128]{2,0,1:T(8,128)(2,1)S(1)} fusion(bf16[512,12,128]{2,1,0:T(8,128)(2,1)} %copy.45, bf16[512,12,128]{2,1,0:T(8,128)(2,1)} %copy.44, bf16[512,12,128]{2,1,0:T(8,128)(2,1)} %copy.43, s32[12]{0:T(128)S(1)} %bitcast.45), kind=kOutput, calls=%fused_computation.2 | convolution fusion | flops 70779024 | bytes 9437232 | tf_op jit(solution)/shard_map/lbk,bj->ljk/dot_general | solution.py:9
  36.9 1.2 copy.58
  38.2 2.2 copy-done.3
  41.2 5.1 %slice_convert_fusion = f32[1024,12,128]{2,0,1:T(8,128)} fusion(bf16[1536,12,128]{2,0,1:T(8,128)(2,1)} %bitcast.35), kind=kLoop, calls=%fused_computation.13 | loop fusion | flops 1572864 | bytes 9437184 | tf_op jit(solution)/shard_map/convert_element_type | solution.py:53
  46.3 6.6 %copy.48 = f32[1024,12,128]{0,2,1:T(8,128)} copy(f32[1024,12,128]{2,0,1:T(8,128)} %slice_convert_fusion) | data formatting | bytes 12582912 | tf_op jit(solution)/shard_map/convert_element_type | solution.py:53
  52.9 6.7 %copy.49 = f32[1024,1536]{1,0:T(8,128)} copy(f32[1024,1536]{0,1:T(8,128)} %bitcast.33) | data formatting | bytes 12582912 | tf_op jit(solution)/shard_map/convert_element_type | solution.py:53
  59.6 4.5 %fusion.13 = f32[1024,1536]{1,0:T(8,128)} fusion(bf16[512,1536]{0,1:T(8,128)(2,1)S(1)} %bitcast.39, bf16[512,512]{1,0:T(8,128)(2,1)S(1)} %bitcast.43, bf16[512,512]{1,0:T(8,128)(2,1)S(1)} %bitcast.44), kind=kOutput, calls=%fused_computation.25 | convolution fusion | flops 1612709888 | bytes 8912896 | tf_op jit(solution)/shard_map/dot_general | solution.py:54
  64.0 46.5 %all-to-all-done = bf16[16,96,1280]{2,1,0:T(8,128)(2,1)} async-done(((bf16[16,96,1280]{2,1,0:T(8,128)(2,1)}), bf16[16,96,1280]{2,1,0:T(8,128)(2,1)}, u32[]{:S(2)}, u32[]{:S(2)}) %all-to-all-start) | async-done | bytes 3932192 | tf_op jit(solution)/shard_map/all_to_all | solution.py:63
  110.6 4.5 %convolution_convert_fusion.1 = bf16[512,1280]{1,0:T(8,128)(2,1)S(1)} fusion(bf16[512,1536]{0,1:T(8,128)(2,1)S(1)} %bitcast.40, bf16[1536,1280]{1,0:T(8,128)(2,1)} %bitcast.12), kind=kOutput, calls=%fused_computation.15 | convolution fusion | flops 2013921280 | bytes 6815744 | tf_op jit(solution)/shard_map/dot_general | solution.py:72
  115.1 1.3 copy-done.4
  116.4 6.6 %convolution_convert_fusion = bf16[1024,1280]{1,0:T(8,128)(2,1)S(1)} fusion(bf16[1536,1280]{1,0:T(8,128)(2,1)} %bitcast.12, f32[1024,1536]{1,0:T(8,128)S(1)} %copy-done.2, f32[1024,1536]{1,0:T(8,128)S(1)} %copy-done.4), kind=kOutput, calls=%fused_computation.11 | convolution fusion | flops 4032561152 | bytes 19136512 | tf_op jit(solution)/shard_map/dot_general | solution.py:73
  123.0 1.3 fusion.18
  124.3 1.3 fusion.21
  125.6 1.4 convolution_add_fusion.2
  127.1 1.4 convolution_add_fusion.3
  128.5 4.1 pad_maximum_fusion
  132.6 2.0 fusion.9
  136.4 1.8 pad_maximum_fusion.1
  138.2 5.7 %fusion.7 = f32[1024,256]{1,0:T(8,128)S(1)} fusion(f32[1024,1536]{1,0:T(8,128)} %fusion.13, f32[1024,1536]{1,0:T(8,128)} %copy.49, bf16[1536,1280]{1,0:T(8,128)(2,1)} %bitcast.12), kind=kOutput, calls=%fused_computation.12 | convolution fusion | flops 808452096 | bytes 14417920 | tf_op jit(solution)/shard_map/dot_general | solution.py:74
  143.9 1.0 slice_bitcast_fusion
  144.9 273.2 %all-reduce.3.cloned.1.call-done = f32[1024,2048]{0,1:T(8,128)} async-done(((f32[1024,2048]{0,1:T(8,128)}), f32[1024,2048]{0,1:T(8,128)}) %all-reduce.3.cloned.1.call-update) | async-done | bytes 8388624
  418.1 1.5 fusion.38
  419.6 0.8 copy.52
  420.4 0.8 copy.51
  421.2 1.6 slice_bitcast_fusion.2
  (32 shorter events, 4.1 us)
Async XLA Ops:
  11.2 9.8 %copy-start.5 = (bf16[1,512,1536]{2,1,0:T(8,128)(2,1)S(1)}, bf16[1,512,1536]{2,1,0:T(8,128)(2,1)}, u32[]{:S(2)}) copy-start(bf16[1,512,1536]{2,1,0:T(8,128)(2,1)} %param.10) | copy-start | bytes 4718596
  11.2 99.4 %all-to-all-start = ((bf16[16,96,1280]{2,1,0:T(8,128)(2,1)}), bf16[16,96,1280]{2,1,0:T(8,128)(2,1)}, u32[]{:S(2)}, u32[]{:S(2)}) async-start(bf16[16,96,1280]{2,1,0:T(8,128)(2,1)} %stack.2), calls=%async_computation | async-start | bytes 7864320 | tf_op jit(solution)/shard_map/all_to_all | solution.py:63
  21.0 397.1 %all-reduce.3.cloned.1.call-start = ((), (), s32[]{:S(2)}) async-start(), calls=%async_computation.3 | async-start | bytes 16777216
  21.7 3.0 copy-start.6
  25.5 3.0 copy-start.7
  29.3 3.0 copy-start.10
  38.2 2.2 copy-start.3
  52.9 6.7 %copy-start.8 = (bf16[1,512,512]{2,1,0:T(8,128)(2,1)S(1)}, bf16[1,512,512]{2,1,0:T(8,128)(2,1)}, u32[]{:S(2)}) copy-start(bf16[1,512,512]{2,1,0:T(8,128)(2,1)} %param.9) | copy-start | bytes 1572868
  52.9 6.7 %copy-start.9 = (bf16[1,512,512]{2,1,0:T(8,128)(2,1)S(1)}, bf16[1,512,512]{2,1,0:T(8,128)(2,1)}, u32[]{:S(2)}) copy-start(bf16[1,512,512]{2,1,0:T(8,128)(2,1)} %param.8) | copy-start | bytes 1572868
  110.6 4.5 %copy-start.2 = (f32[1024,1536]{1,0:T(8,128)S(1)}, f32[1024,1536]{1,0:T(8,128)}, u32[]{:S(2)}) copy-start(f32[1024,1536]{1,0:T(8,128)} %copy.49) | copy-start | bytes 18874372
  110.6 5.8 %copy-start.4 = (f32[1024,1536]{1,0:T(8,128)S(1)}, f32[1024,1536]{1,0:T(8,128)}, u32[]{:S(2)}) copy-start(f32[1024,1536]{1,0:T(8,128)} %fusion.13) | copy-start | bytes 18874372
  123.0 4.1 copy-start
  132.6 288.6 %reduce-scatter.3.cloned.1.call-start = ((), (), s32[]{:S(2)}) async-start(), calls=%async_computation.2 | async-start | bytes 2785280 | tf_op jit(solution)/shard_map/reduce_scatter | solution.py:92
  132.6 2.1 copy-start.1
Sparse Core Ops, SparseCore 0:
  132.7 285.3 all-reduce.2
Sparse Core Ops, SparseCore 1:
  138.2 79.0 reduce-scatter.2
